TPU v7x, 128 devices: a whole 4x4x4 slice. The times are simulated.
128 devices in a mesh: pool: 4 (over x_hi, core), grp: 4 (over y), tp: 8 (over z, x_lo).
Axes of the slice: x: 4 (x_hi: 2, x_lo: 2; x = x_hi * 2 + x_lo), y: 4, z: 4, core: 2. Of those that a mesh axis runs over, the one named last changes fastest.
Arguments:
- hidden: bfloat16 [1024, 8192], P('pool', 'grp'), may hold values from -6 to 6
- attn_gain: float32 [8192], P('grp'), may hold values from 0.25 to 1.75
- w_query: bfloat16 [8192, 8192], P('grp', 'tp'), may hold values from -0.0625 to 0.0625
- w_key: bfloat16 [8192, 1024], P('grp', 'tp'), may hold values from -1 to 1
- w_value: bfloat16 [8192, 1024], P('grp', 'tp'), may hold values from -0.0625 to 0.0625
- w_out: bfloat16 [8192, 8192], P('tp', 'grp'), may hold values from -0.0625 to 0.0625
- prefix_keys: bfloat16 [8, 16384, 1024], P('pool', 'grp', 'tp'), may hold values from -300 to 300
- prefix_values: bfloat16 [8, 16384, 1024], P('pool', 'grp', 'tp'), may hold values from -6 to 6
- suffix_keys: bfloat16 [1024, 256, 1024], P('pool', 'grp', 'tp'), may hold values from -300 to 300
- suffix_values: bfloat16 [1024, 256, 1024], P('pool', 'grp', 'tp'), may hold values from -6 to 6
- prefix_ids: int32 [1024], P('pool'), may hold values from 0 to 7, as said below
- suffix_lens: int32 [1024], P('pool'), may hold values from 1 to 256, as said below
- ffn_gain: float32 [8192], P('grp'), may hold values from 0.25 to 1.75
- w_gate: bfloat16 [8192, 14336], P('grp', ('pool', 'tp')), may hold values from -0.0625 to 0.0625
- w_up: bfloat16 [8192, 14336], P('grp', ('pool', 'tp')), may hold values from -0.0625 to 0.0625
- w_down: bfloat16 [14336, 8192], P(('pool', 'tp'), 'grp'), may hold values from -0.046875 to 0.046875
Outputs:
- result: bfloat16 [1024, 8192], P(('pool', 'tp'), 'grp')
Inputs may be any that keep to these rules, and one draw needn't show every extreme that they name: `prefix_ids`: within rows p * 256 to (p + 1) * 256 - 1, each of the prefixes p * 2 to (p + 1) * 2 - 1 is named by exactly 128 streams, and no other prefix is named. `suffix_lens`: each block of 256 streams holds a stream of length 256 and one of length 1.
All inputs are finite; a program needn't handle non-finite values.
Results may differ from a plain program's by a relative error of at most 0.015.
Values may be sent and summed in bfloat16 or wider, within the bound.
No kernel may reach another device: no remote copies, remote signals or barrier semaphores. Data moves between devices by JAX's collectives and lax.ppermute only.
A program may use at most 192 MiB of HBM per device.

v0:
```python
import math
import jax
import jax.numpy as jnp
from jax import lax
from jax.sharding import PartitionSpec as P

D = 8192
HD = 128
epsilon = 1e-05


def joined(array, axis, combine):
    everything = jax.tree.map(lambda part: lax.all_gather(part, axis), array)
    first = jax.tree.map(lambda part: part[0], everything)

    def lap(k, so_far):
        return combine(so_far, jax.tree.map(lambda part: part[k], everything))

    return lax.fori_loop(1, lax.axis_size(axis), lap, first)


def combine_parts(earlier, later):
    peak_one, total_one, numer_one = earlier
    peak_two, total_two, numer_two = later
    peak = jnp.maximum(peak_one, peak_two)
    scale_one = jnp.exp(peak_one - peak)
    scale_two = jnp.exp(peak_two - peak)
    total = total_one * scale_one + total_two * scale_two
    numer = numer_one * scale_one[..., None] + numer_two * scale_two[..., None]
    return (peak, total, numer)


def body(
    hidden,
    attn_gain,
    w_query,
    w_key,
    w_value,
    w_out,
    prefix_keys,
    prefix_values,
    suffix_keys,
    suffix_values,
    prefix_ids,
    suffix_lens,
    ffn_gain,
    w_gate,
    w_up,
    w_down,
):
    stream_count = hidden.shape[0]
    hidden_float = hidden.astype(jnp.float32)
    squares = lax.psum(jnp.sum(hidden_float * hidden_float, axis=1), "grp")
    inverse = lax.rsqrt(squares / D + epsilon)
    normed = (hidden_float * inverse[:, None] * attn_gain).astype(jnp.bfloat16)
    part_query = jnp.dot(normed, w_query, preferred_element_type=jnp.float32)
    part_key = jnp.dot(normed, w_key, preferred_element_type=jnp.float32)
    part_value = jnp.dot(normed, w_value, preferred_element_type=jnp.float32)
    query, key_new, value_new = lax.psum((part_query, part_key, part_value), "grp")
    query = query.astype(jnp.bfloat16)
    key_new = key_new.astype(jnp.bfloat16)
    value_new = value_new.astype(jnp.bfloat16)
    kv_local = w_key.shape[1] // HD
    q_local = w_query.shape[1] // HD
    groups = q_local // kv_local
    prefix_local = prefix_keys.shape[0]
    pre_length = prefix_keys.shape[1]
    suf_length = suffix_keys.shape[1]
    factor = 1.0 / math.sqrt(HD)
    heads = query.reshape(stream_count, kv_local, groups, HD)
    pre_key = prefix_keys.reshape(prefix_local, pre_length, kv_local, HD)
    pre_value = prefix_values.reshape(prefix_local, pre_length, kv_local, HD)
    suf_key = suffix_keys.reshape(stream_count, suf_length, kv_local, HD)
    suf_value = suffix_values.reshape(stream_count, suf_length, kv_local, HD)
    local_prefix = prefix_ids - lax.axis_index("pool") * prefix_local
    per_group = stream_count // prefix_local
    one_hot = (local_prefix[:, None] == jnp.arange(prefix_local, dtype=jnp.int32)[None, :]).astype(
        jnp.int32
    )
    rank_within = jnp.sum(jnp.cumsum(one_hot, axis=0) * one_hot, axis=1) - 1
    target = local_prefix * per_group + rank_within
    group_order = (
        jnp.zeros((stream_count,), jnp.int32)
        .at[target]
        .set(jnp.arange(stream_count, dtype=jnp.int32))
    )
    grouped = heads[group_order].reshape(prefix_local, per_group, kv_local, groups, HD)
    pre_scores = (
        jnp.einsum("pskgd,pjkd->pskgj", grouped, pre_key, preferred_element_type=jnp.float32)
        * factor
    )
    pre_peak = pre_scores.max(axis=4).reshape(stream_count, kv_local, groups)[target]
    positions = lax.axis_index("grp") * suf_length + jnp.arange(suf_length, dtype=jnp.int32)
    valid = (positions[None, :] < suffix_lens[:, None])[:, None, None, :]
    suf_scores = (
        jnp.einsum("skgd,sjkd->skgj", heads, suf_key, preferred_element_type=jnp.float32) * factor
    )
    suf_scores = jnp.where(valid, suf_scores, -1e30)
    peak = jnp.maximum(pre_peak, suf_scores.max(axis=3))
    peak_grouped = peak[group_order].reshape(prefix_local, per_group, kv_local, groups)
    pre_weights = jnp.exp(pre_scores - peak_grouped[..., None]).astype(jnp.bfloat16)
    pre_total = (
        pre_weights.astype(jnp.float32).sum(axis=4).reshape(stream_count, kv_local, groups)[target]
    )
    pre_numer = jnp.einsum(
        "pskgj,pjkd->pskgd", pre_weights, pre_value, preferred_element_type=jnp.float32
    )
    pre_numer = pre_numer.reshape(stream_count, kv_local, groups, HD)[target]
    suf_weights = jnp.where(valid, jnp.exp(suf_scores - peak[:, :, :, None]), 0.0).astype(
        jnp.bfloat16
    )
    total = pre_total + suf_weights.astype(jnp.float32).sum(axis=3)
    numer = pre_numer + jnp.einsum(
        "skgj,sjkd->skgd", suf_weights, suf_value, preferred_element_type=jnp.float32
    )
    peak, total, numer = joined((peak, total, numer), "grp", combine_parts)
    own_score = (
        jnp.einsum(
            "skgd,skd->skg",
            heads,
            key_new.reshape(stream_count, kv_local, HD),
            preferred_element_type=jnp.float32,
        )
        * factor
    )
    new_peak = jnp.maximum(peak, own_score)
    rescale = jnp.exp(peak - new_peak)
    own_weight = jnp.exp(own_score - new_peak).astype(jnp.bfloat16).astype(jnp.float32)
    total = total * rescale + own_weight
    own_value = value_new.reshape(stream_count, kv_local, 1, HD).astype(jnp.float32)
    numer = numer * rescale[..., None] + own_weight[..., None] * own_value
    attended = (numer / total[..., None]).reshape(stream_count, q_local * HD).astype(jnp.bfloat16)
    partial_out = jnp.dot(attended, w_out, preferred_element_type=jnp.float32)
    share = stream_count // lax.axis_size("tp")
    tp_start = lax.axis_index("tp") * share
    summed = lax.psum(partial_out, "tp")
    summed = lax.dynamic_slice_in_dim(summed, tp_start, share, 0)
    own_hidden = lax.dynamic_slice_in_dim(hidden_float, tp_start, share, 0)
    middle = (own_hidden + summed).astype(jnp.bfloat16)
    gathered = lax.all_gather(middle, ("pool", "tp"), axis=0, tiled=True)
    gathered_float = gathered.astype(jnp.float32)
    ffn_squares = lax.psum(jnp.sum(gathered_float * gathered_float, axis=1), "grp")
    ffn_inverse = lax.rsqrt(ffn_squares / D + epsilon)
    normed_ffn = (gathered_float * ffn_inverse[:, None] * ffn_gain).astype(jnp.bfloat16)
    part_gate = jnp.dot(normed_ffn, w_gate, preferred_element_type=jnp.float32)
    part_upward = jnp.dot(normed_ffn, w_up, preferred_element_type=jnp.float32)
    gate, upward = lax.psum((part_gate, part_upward), "grp")
    act = (jax.nn.silu(gate) * upward).astype(jnp.bfloat16)
    returned = lax.psum_scatter(
        jnp.dot(act, w_down, preferred_element_type=jnp.float32),
        ("pool", "tp"),
        scatter_dimension=0,
        tiled=True,
    )
    return (middle.astype(jnp.float32) + returned).astype(jnp.bfloat16)


def solution(mesh):
    return jax.shard_map(
        body,
        mesh=mesh,
        in_specs=(
            P("pool", "grp"),
            P("grp"),
            P("grp", "tp"),
            P("grp", "tp"),
            P("grp", "tp"),
            P("tp", "grp"),
            P("pool", "grp", "tp"),
            P("pool", "grp", "tp"),
            P("pool", "grp", "tp"),
            P("pool", "grp", "tp"),
            P("pool"),
            P("pool"),
            P("grp"),
            P("grp", ("pool", "tp")),
            P("grp", ("pool", "tp")),
            P(("pool", "tp"), "grp"),
        ),
        out_specs=P(("pool", "tp"), "grp"),
        check_vma=False,
    )
```

profile of v0, /device:TPU:1, one launch (start us, length us, event | category | flops | bytes accessed | tf_op | source)
XLA Modules:
  0.0 672.8 jit_solution(15598244335575411505)
XLA Ops:
  6.5 0.8 fusion.59
  7.4 0.7 broadcast_subtract_fusion
  8.1 1.6 multiply_reduce_fusion
  9.7 9.5 %psum.56 = f32[256]{0:T(256)S(1)} all-reduce(f32[256]{0:T(256)S(1)} %multiply_reduce_fusion), channel_id=1, replica_groups=mesh['pool'=4,'grp'=4,'tp'=8] {'grp'}, use_global_device_ids=true, to_apply=%region_1.0 | all-reduce | flops 256 | bytes 2048 | tf_op jit(solution)/shard_map/psum | solution.py:53
  19.2 4.9 fusion.46
  24.1 0.5 fusion.45
  24.7 0.5 fusion.44
  25.2 26.5 %all-reduce.9 = (bf16[256,1024]{1,0:T(8,128)(2,1)S(1)}, bf16[256,128]{1,0:T(8,128)(2,1)S(1)}, bf16[256,128]{1,0:T(8,128)(2,1)S(1)}) all-reduce(f32[256,1024]{1,0:T(8,128)} %fusion.46, f32[256,128]{1,0:T(8,128)S(1)} %fusion.45, f32[256,128]{1,0:T(8,128)S(1)} %fusion.44), channel_id=1, replica_groups=mesh['pool'=4,'grp'=4,'tp'=8] {'grp'}, use_global_device_ids=true, to_apply=%region_2.0 | all-reduce | flops 327680 | bytes 1966080 | tf_op jit(solution)/shard_map/psum | solution.py:59
  51.7 0.1 copy.64
  51.8 0.6 reduce-window.6
  52.4 0.2 slice_reduce_fusion
  52.6 0.2 reduce-window.9
  52.8 0.1 add_bitcast_fusion
  53.0 1.6 scatter_custom_fusion
  54.6 0.8 gather_fusion
  55.4 13.1 %bitcast_reduce_fusion = (f32[2,128,8]{1,2,0:T(8,128)S(1)}, f32[2,128,8,4096]{3,1,2,0:T(8,128)}) fusion(bf16[2,4096,128]{2,1,0:T(8,128)(2,1)S(1)} %copy-done, bf16[2,128,8,128]{3,2,1,0:T(8,128)(2,1)S(1)} %bitcast.165), kind=kOutput, calls=%fused_computation.17 | convolution fusion | flops 2164258816 | bytes 36184064 | tf_op jit(solution)/shard_map/pskgd,pjkd->pskgj/dot_general | solution.py:89
  68.5 0.1 copy.47
  68.6 0.7 gather_fusion.1
  69.4 0.1 broadcast_compare_fusion
  69.5 4.5 fusion.47
  74.1 0.7 gather_fusion.2
  74.9 13.8 %fusion.17 = f32[2,128,1,8,128]{4,1,3,0,2:T(8,128)S(1)} fusion(bf16[2,4096,128]{2,1,0:T(8,128)(2,1)} %param.25, f32[2,128,8]{1,2,0:T(8,128)S(1)} %copy.48, f32[2,128,8,4096]{3,1,2,0:T(8,128)} %get-tuple-element.234), kind=kOutput, calls=%fused_computation.37 | convolution fusion | flops 2172649472 | bytes 36708352 | tf_op jit(solution)/shard_map/pskgj,pjkd->pskgd/dot_general | solution.py:105
  88.7 1.6 copy.50
  90.3 2.9 gather_fusion.4
  93.2 4.7 convolution_add_fusion
  98.0 10.4 %all-gather.1 = f32[1024,8]{1,0:T(8,128)S(1)} all-gather(f32[256,8]{1,0:T(8,128)S(1)} %max.43), channel_id=3, replica_groups=mesh['pool'=4,'grp'=4,'tp'=8] {'grp'}, dimensions={0}, use_global_device_ids=true | all-gather | bytes 40960 | tf_op jit(solution)/shard_map/all_gather | solution.py:13
  108.5 14.6 %convert_reduce_fusion = f32[2,128,8]{1,2,0:T(8,128)S(1)} fusion(f32[2,128,8]{1,2,0:T(8,128)S(1)} %copy.48, f32[2,128,8,4096]{3,1,2,0:T(8,128)} %get-tuple-element.234), kind=kLoop, calls=%fused_computation.20 | loop fusion | flops 41940992 | bytes 33570816 | tf_op jit(solution)/shard_map/reduce_sum | solution.py:103
  123.2 0.1 copy.49
  123.3 0.7 gather_fusion.3
  124.0 0.7 convert_reduce_fusion.1
  124.8 14.8 %all-gather.2 = f32[1024,8]{1,0:T(8,128)S(1)} all-gather(f32[256,8]{1,0:T(8,128)S(1)} %add.162), channel_id=4, replica_groups=mesh['pool'=4,'grp'=4,'tp'=8] {'grp'}, dimensions={0}, use_global_device_ids=true | all-gather | bytes 40960 | tf_op jit(solution)/shard_map/all_gather | solution.py:13
  139.7 0.2 copy.54
  139.8 0.2 copy.55
  140.0 0.4 fusion.32
  140.4 0.1 copy.63
  140.5 16.9 %all-gather.8.cloned.1.call-done = f32[1024,8,128]{2,1,0:T(8,128)} async-done(((f32[256,8,128]{2,1,0:T(8,128)}), f32[1024,8,128]{2,1,0:T(8,128)}) %all-gather.8.cloned.1.call-update) | async-done | bytes 4194320 | tf_op jit(solution)/shard_map/all_gather | solution.py:13
  157.4 1.3 slice_bitcast_fusion
  158.7 6.7 while.19
  158.8 0.1 copy.80
  158.9 0.1 copy.81
  159.0 1.9 fusion.65
  161.0 0.1 copy.80
  161.1 0.1 copy.81
  161.3 1.9 fusion.65
  163.3 0.1 copy.80
  163.4 0.1 copy.81
  163.5 1.9 fusion.65
  165.4 0.1 copy.59
  165.6 0.1 copy.58
  165.7 0.1 copy.57
  165.8 1.0 divide_convert_fusion
  166.9 4.8 fusion.28
  171.8 1.6 convert_element_type.68
  173.4 103.1 %all-reduce.6.cloned.1.call-done = f32[256,2048]{1,0:T(8,128)} async-done(((f32[256,2048]{1,0:T(8,128)}), f32[256,2048]{1,0:T(8,128)}) %all-reduce.6.cloned.1.call-update) | async-done | bytes 2097168 | tf_op jit(solution)/shard_map/psum | solution.py:136
  276.5 1.7 add_convert_fusion.1
  278.2 85.9 %all-gather.6.cloned.1.call-done = bf16[1024,2048]{1,0:T(8,128)(2,1)} async-done(((bf16[32,2048]{1,0:T(8,128)(2,1)}), bf16[1024,2048]{1,0:T(8,128)(2,1)}) %all-gather.6.cloned.1.call-update) | async-done | bytes 4194320 | tf_op jit(solution)/shard_map/all_gather | solution.py:140
  364.2 3.1 fusion.9
  367.2 8.5 %psum.61 = f32[1024]{0:T(1024)S(1)} all-reduce(f32[1024]{0:T(1024)S(1)} %fusion.9), channel_id=1, replica_groups=mesh['pool'=4,'grp'=4,'tp'=8] {'grp'}, use_global_device_ids=true, to_apply=%region_17.18 | all-reduce | flops 1024 | bytes 8192 | tf_op jit(solution)/shard_map/psum | solution.py:142
  375.7 6.4 fusion.22
  382.1 3.5 fusion.24
  385.6 85.0 %all-reduce.8.cloned.1.call-done = (f32[1024,448]{0,1:T(8,128)}, f32[1024,448]{0,1:T(8,128)}) async-done(((f32[1024,448]{0,1:T(8,128)}, f32[1024,448]{0,1:T(8,128)}), (f32[1024,448]{0,1:T(8,128)}, f32[1024,448]{0,1:T(8,128)})) %all-reduce.8.cloned.1.call-update) | async-done | bytes 3670032 | tf_op jit(solution)/shard_map/psum | solution.py:147
  470.7 8.3 %fusion.26 = f32[1024,2048]{1,0:T(8,128)} fusion(bf16[448,2048]{1,0:T(8,128)(2,1)} %param.33, f32[1024,448]{0,1:T(8,128)} %get-tuple-element.224, f32[1024,448]{0,1:T(8,128)} %get-tuple-element.225), kind=kOutput, calls=%fused_computation.44 | convolution fusion | flops 1881800704 | bytes 13893632 | tf_op jit(solution)/shard_map/dot_general | solution.py:150
  478.9 185.7 %reduce-scatter.2.cloned.1.call-done = f32[32,2048]{1,0:T(8,128)} async-done(((f32[1024,2048]{1,0:T(8,128)}), f32[32,2048]{1,0:T(8,128)}) %reduce-scatter.2.cloned.1.call-update) | async-done | bytes 262160 | tf_op jit(solution)/shard_map/reduce_scatter | solution.py:149
  664.6 1.6 add_convert_fusion
  (64 shorter events, 0.8 us)
Async XLA Ops:
  6.5 48.9 %copy-start = (bf16[2,4096,128]{2,1,0:T(8,128)(2,1)S(1)}, bf16[2,4096,128]{2,1,0:T(8,128)(2,1)}, u32[]{:S(2)}) copy-start(bf16[2,4096,128]{2,1,0:T(8,128)(2,1)} %param.24) | copy-start | bytes 6291460
  6.5 150.9 %all-gather.8.cloned.1.call-start = ((), (), s32[]{:S(2)}) async-start(), calls=%async_computation.4 | async-start | bytes 5242880 | tf_op jit(solution)/shard_map/all_gather | solution.py:13
  8.1 16.1 %copy-start.2 = (bf16[256,2048]{1,0:T(8,128)(2,1)S(1)}, bf16[256,2048]{1,0:T(8,128)(2,1)}, u32[]{:S(2)}) copy-start(bf16[256,2048]{1,0:T(8,128)(2,1)} %param.18) | copy-start | bytes 3145732
  8.1 16.1 %copy-start.11 = (f32[2048]{0:T(1024)S(1)}, f32[2048]{0:T(1024)}, u32[]{:S(2)}) copy-start(f32[2048]{0:T(1024)} %param.19) | copy-start | bytes 24580
  19.2 4.9 copy-start.9
  19.2 5.4 copy-start.10
  24.1 28.8 %copy-start.6 = (s32[256]{0:T(256)S(1)}, s32[256]{0:T(256)}, u32[]{:S(2)}) copy-start(s32[256]{0:T(256)} %param.28) | copy-start | bytes 3076
  55.4 14.0 %copy-start.7 = (s32[256]{0:T(256)S(1)}, s32[256]{0:T(256)}, u32[]{:S(2)}) copy-start(s32[256]{0:T(256)} %param.29) | copy-start | bytes 3076
  98.0 178.5 %all-reduce.6.cloned.1.call-start = ((), (), s32[]{:S(2)}) async-start(), calls=%async_computation.1 | async-start | bytes 4194304 | tf_op jit(solution)/shard_map/psum | solution.py:136
  166.8 4.9 copy-start.3
  171.7 204.0 %copy-start.12 = (f32[2048]{0:T(1024)S(1)}, f32[2048]{0:T(1024)}, u32[]{:S(2)}) copy-start(f32[2048]{0:T(1024)} %param.30) | copy-start | bytes 24580
  171.7 192.4 %all-gather.6.cloned.1.call-start = ((), (), s32[]{:S(2)}) async-start(), calls=%async_computation.2 | async-start | bytes 4325376 | tf_op jit(solution)/shard_map/all_gather | solution.py:140
  278.2 192.5 %all-reduce.8.cloned.1.call-start = ((), (), s32[]{:S(2)}) async-start(), calls=%async_computation.5 | async-start | bytes 7340032 | tf_op jit(solution)/shard_map/psum | solution.py:147
  375.7 6.4 copy-start.4
  375.7 6.4 copy-start.8
  385.6 279.0 %reduce-scatter.2.cloned.1.call-start = ((), (), s32[]{:S(2)}) async-start(), calls=%async_computation.3 | async-start | bytes 8650752 | tf_op jit(solution)/shard_map/reduce_scatter | solution.py:149
  478.9 187.3 %copy-start.1 = (bf16[2,4096,128]{2,1,0:T(8,128)(2,1)S(1)}, bf16[2,4096,128]{2,1,0:T(8,128)(2,1)}, u32[]{:S(2)}) copy-start(bf16[2,4096,128]{2,1,0:T(8,128)(2,1)} %param.24) | copy-start | bytes 6291460
  478.9 185.7 %copy-start.5 = (bf16[32,2048]{1,0:T(8,128)(2,1)S(1)}, bf16[32,2048]{1,0:T(8,128)(2,1)}, u32[]{:S(2)}) copy-start(bf16[32,2048]{1,0:T(8,128)(2,1)} %add_convert_fusion.1) | copy-start | bytes 393220
Sparse Core Ops, SparseCore 0:
  98.1 59.2 all-gather.7
  171.8 104.5 all-reduce.5
  278.3 85.8 all-gather.5
  385.7 84.8 all-reduce.7
  479.1 185.5 reduce-scatter.1
where the time goes:
time: 673 us
  waiting for transfers between devices  477 us (71%)
  blocking collectives  69.7 us (10%)
  matrix products  65.4 us (10%)
  other arithmetic  34.3 us (5%)
  between operations  13.5 us (2%)
  local copies, waits for them, and re-layouts  12.8 us (2%)
    reduce_scatter x1, waiting for transfers between devices, body(): lax.psum_scatter(jnp.dot(act, w_down, preferred_element_type=jnp.float32)...  186 us
    psum x1, waiting for transfers between devices, body(): summed = lax.psum(partial_out, 'tp')  103 us
    all_gather x1, waiting for transfers between devices, body(): gathered = lax.all_gather(middle, ('pool', 'tp'), axis=0, tiled=True)  85.9 us
    psum x1, waiting for transfers between devices, body(): gate, upward = lax.psum((part_gate, part_upward), 'grp')  85 us
    psum x1, blocking collectives, body(): lax.psum((part_query, part_key, part_value), 'grp')  26.5 us
    all_gather x2, blocking collectives, joined(): everything = jax.tree.map(lambda part: lax.all_gather(part, axis), array)  25.2 us
    all_gather x1, waiting for transfers between devices, joined(): everything = jax.tree.map(lambda part: lax.all_gather(part, axis), array)  16.9 us
    reduce_sum x1, other arithmetic, body(): pre_weights.astype(jnp.float32).sum(axis=4)  14.6 us
  transfers between devices with their start and end apart: 5, of which 5 were waited for; matrix products, arithmetic and copies ran while one was open for 3% of the time, Pallas kernels for 0%

commit v1 on v0

--- a/solution.py
+++ b/solution.py
@@ -137,7 +137,10 @@
     summed = lax.dynamic_slice_in_dim(summed, tp_start, share, 0)
     own_hidden = lax.dynamic_slice_in_dim(hidden_float, tp_start, share, 0)
     middle = (own_hidden + summed).astype(jnp.bfloat16)
-    gathered = lax.all_gather(middle, ("pool", "tp"), axis=0, tiled=True)
+    gathered = jnp.concatenate(
+        lax.all_to_all(jnp.stack([middle] * lax.axis_size(("pool", "tp"))), ("pool", "tp"), 0, 0),
+        axis=0,
+    )
     gathered_float = gathered.astype(jnp.float32)
     ffn_squares = lax.psum(jnp.sum(gathered_float * gathered_float, axis=1), "grp")
     ffn_inverse = lax.rsqrt(ffn_squares / D + epsilon)

time: 673 us -> 640 us (0.951)
  waiting for transfers between devices: 477 us -> 388 us
  blocking collectives: 69.7 us -> 125 us
    all_gather x1 -> x0, waiting for transfers between devices: 85.9 us -> none  [body(): gathered = lax.all_gather(middle, ('pool', 'tp'), axis=0, tiled=True)]
    all_to_all x0 -> x1, blocking collectives: none -> 55.8 us  [body(): lax.all_to_all(jnp.stack([middle] * lax.axis_size(('pool', 'tp'))), ('poo...]
  transfers between devices with their start and end apart: 5 -> 4, of which waited for: 5 -> 4; matrix products, arithmetic and copies ran while one was open for 3% -> 3% of each run, Pallas kernels for 0% -> 0%
where the time goes in v1:
time: 640 us
  waiting for transfers between devices  388 us (61%)
  blocking collectives  125 us (20%)
  matrix products  61.8 us (10%)
  other arithmetic  34.9 us (5%)
  local copies, waits for them, and re-layouts  15.3 us (2%)
  between operations  13.5 us (2%)
    reduce_scatter x1, waiting for transfers between devices, body(): lax.psum_scatter(jnp.dot(act, w_down, preferred_element_type=jnp.float32)...  186 us
    psum x1, waiting for transfers between devices, body(): summed = lax.psum(partial_out, 'tp')  103 us
    psum x1, waiting for transfers between devices, body(): gate, upward = lax.psum((part_gate, part_upward), 'grp')  82.5 us
    all_to_all x1, blocking collectives, body(): lax.all_to_all(jnp.stack([middle] * lax.axis_size(('pool', 'tp'))), ('poo...  55.8 us
    psum x1, blocking collectives, body(): lax.psum((part_query, part_key, part_value), 'grp')  26.5 us
    all_gather x2, blocking collectives, joined(): everything = jax.tree.map(lambda part: lax.all_gather(part, axis), array)  25.2 us
    all_gather x1, waiting for transfers between devices, joined(): everything = jax.tree.map(lambda part: lax.all_gather(part, axis), array)  16.9 us
    reduce_sum x1, other arithmetic, body(): pre_weights.astype(jnp.float32).sum(axis=4)  14.6 us
  transfers between devices with their start and end apart: 4, of which 4 were waited for; matrix products, arithmetic and copies ran while one was open for 3% of the time, Pallas kernels for 0%

profile of v1, /device:TPU:1, one launch (start us, length us, event | category | flops | bytes accessed | tf_op | source)
XLA Modules:
  0.0 639.7 jit_solution(17779373161029489101)
XLA Ops:
  6.5 0.8 fusion.58
  7.4 0.7 broadcast_subtract_fusion
  8.1 1.6 multiply_reduce_fusion.1
  9.7 9.5 %psum.56 = f32[256]{0:T(256)S(1)} all-reduce(f32[256]{0:T(256)S(1)} %multiply_reduce_fusion.1), channel_id=1, replica_groups=mesh['pool'=4,'grp'=4,'tp'=8] {'grp'}, use_global_device_ids=true, to_apply=%region_1.0 | all-reduce | flops 256 | bytes 2048 | tf_op jit(solution)/shard_map/psum | solution.py:53
  19.2 4.9 fusion.41
  24.1 0.5 fusion.40
  24.7 0.5 fusion.39
  25.2 26.5 %all-reduce.9 = (bf16[256,1024]{1,0:T(8,128)(2,1)S(1)}, bf16[256,128]{1,0:T(8,128)(2,1)S(1)}, bf16[256,128]{1,0:T(8,128)(2,1)S(1)}) all-reduce(f32[256,1024]{1,0:T(8,128)} %fusion.41, f32[256,128]{1,0:T(8,128)S(1)} %fusion.40, f32[256,128]{1,0:T(8,128)S(1)} %fusion.39), channel_id=1, replica_groups=mesh['pool'=4,'grp'=4,'tp'=8] {'grp'}, use_global_device_ids=true, to_apply=%region_2.0 | all-reduce | flops 327680 | bytes 1966080 | tf_op jit(solution)/shard_map/psum | solution.py:59
  51.8 0.6 reduce-window.6
  52.4 0.2 slice_reduce_fusion
  52.6 0.2 reduce-window.9
  53.0 1.6 scatter_custom_fusion
  54.6 0.8 gather_fusion
  55.4 13.1 %bitcast_reduce_fusion = (f32[2,128,8]{1,2,0:T(8,128)S(1)}, f32[2,128,8,4096]{3,1,2,0:T(8,128)}) fusion(bf16[2,4096,128]{2,1,0:T(8,128)(2,1)S(1)} %copy-done, bf16[2,128,8,128]{3,2,1,0:T(8,128)(2,1)S(1)} %bitcast.173), kind=kOutput, calls=%fused_computation.17 | convolution fusion | flops 2164258816 | bytes 36184064 | tf_op jit(solution)/shard_map/pskgd,pjkd->pskgj/dot_general | solution.py:89
  68.5 0.1 copy.63
  68.6 0.7 gather_fusion.1
  69.5 4.5 fusion.42
  74.1 0.7 gather_fusion.2
  74.9 13.8 %fusion.16 = f32[2,128,1,8,128]{4,1,3,0,2:T(8,128)S(1)} fusion(bf16[2,4096,128]{2,1,0:T(8,128)(2,1)} %param.25, f32[2,128,8]{1,2,0:T(8,128)S(1)} %copy.64, f32[2,128,8,4096]{3,1,2,0:T(8,128)} %get-tuple-element.241), kind=kOutput, calls=%fused_computation.36 | convolution fusion | flops 2172649472 | bytes 36708352 | tf_op jit(solution)/shard_map/pskgj,pjkd->pskgd/dot_general | solution.py:105
  88.7 1.6 copy.66
  90.3 2.9 gather_fusion.4
  93.2 4.7 convolution_add_fusion
  98.0 10.4 %all-gather.1 = f32[1024,8]{1,0:T(8,128)S(1)} all-gather(f32[256,8]{1,0:T(8,128)S(1)} %max.43), channel_id=3, replica_groups=mesh['pool'=4,'grp'=4,'tp'=8] {'grp'}, dimensions={0}, use_global_device_ids=true | all-gather | bytes 40960 | tf_op jit(solution)/shard_map/all_gather | solution.py:13
  108.5 14.6 %convert_reduce_fusion = f32[2,128,8]{1,2,0:T(8,128)S(1)} fusion(f32[2,128,8]{1,2,0:T(8,128)S(1)} %copy.64, f32[2,128,8,4096]{3,1,2,0:T(8,128)} %get-tuple-element.241), kind=kLoop, calls=%fused_computation.20 | loop fusion | flops 41940992 | bytes 33570816 | tf_op jit(solution)/shard_map/reduce_sum | solution.py:103
  123.2 0.1 copy.65
  123.3 0.7 gather_fusion.3
  124.0 0.7 convert_reduce_fusion.1
  124.8 14.8 %all-gather.2 = f32[1024,8]{1,0:T(8,128)S(1)} all-gather(f32[256,8]{1,0:T(8,128)S(1)} %add.162), channel_id=4, replica_groups=mesh['pool'=4,'grp'=4,'tp'=8] {'grp'}, dimensions={0}, use_global_device_ids=true | all-gather | bytes 40960 | tf_op jit(solution)/shard_map/all_gather | solution.py:13
  139.7 0.2 copy.70
  139.8 0.2 copy.71
  140.0 0.4 fusion.27
  140.5 16.9 %all-gather.5.cloned.1.call-done = f32[1024,8,128]{2,1,0:T(8,128)} async-done(((f32[256,8,128]{2,1,0:T(8,128)}), f32[1024,8,128]{2,1,0:T(8,128)}) %all-gather.5.cloned.1.call-update) | async-done | bytes 4194320 | tf_op jit(solution)/shard_map/all_gather | solution.py:13
  157.4 1.3 slice_bitcast_fusion
  158.7 6.7 %while.19 = (s32[]{:T(128)}, f32[256,1,8]{0,2,1:T(8,128)S(1)}, f32[256,1,8]{0,2,1:T(8,128)S(1)}, f32[256,1,8,128]{3,2,1,0:T(8,128)S(1)}, f32[4,256,1,8]{1,3,2,0:...) while((s32[]{:T(128)}, f32[256,1,8]{0,2,1:T(8,128)S(1)}, ...), condition=%wide.region_12.13_spmd, body=%wide.region_11.12_spmd.sunk | while | flops 800773 | bytes 3301531 | solution.py:19
  158.8 0.1 copy.96
  158.9 0.1 copy.97
  159.0 1.9 fusion.64
  161.0 0.1 copy.96
  161.1 0.1 copy.97
  161.3 1.9 fusion.64
  163.3 0.1 copy.96
  163.4 0.1 copy.97
  163.5 1.9 fusion.64
  165.4 0.1 copy.75
  165.6 0.1 copy.74
  165.7 0.1 copy.73
  165.8 1.0 divide_convert_fusion
  166.9 4.8 fusion.23
  171.8 1.6 convert_element_type.74
  173.3 103.1 %all-reduce.6.cloned.1.call-done = f32[256,2048]{1,0:T(8,128)} async-done(((f32[256,2048]{1,0:T(8,128)}), f32[256,2048]{1,0:T(8,128)}) %all-reduce.6.cloned.1.call-update) | async-done | bytes 2097168 | tf_op jit(solution)/shard_map/psum | solution.py:136
  276.5 1.1 add_convert_fusion.1
  277.5 0.5 stack.2
  278.0 55.8 %all_to_all.5 = bf16[32,32,2048]{2,1,0:T(8,128)(2,1)S(1)} all-to-all(bf16[32,32,2048]{2,1,0:T(8,128)(2,1)S(1)} %stack.2), channel_id=1, replica_groups=mesh['pool'=4,'grp'=4,'tp'=8] {'pool','tp'}, dimensions={0} | all-to-all | bytes 8388608 | tf_op jit(solution)/shard_map/all_to_all | solution.py:141
  333.8 1.9 copy-done.2
  335.7 0.9 multiply_reduce_fusion
  336.7 8.4 %psum.61 = f32[1024]{0:T(1024)S(1)} all-reduce(f32[1024]{0:T(1024)S(1)} %reduce_sum.55), channel_id=1, replica_groups=mesh['pool'=4,'grp'=4,'tp'=8] {'grp'}, use_global_device_ids=true, to_apply=%region_17.18 | all-reduce | flops 1024 | bytes 8192 | tf_op jit(solution)/shard_map/psum | solution.py:145
  345.1 3.3 fusion.10
  348.5 3.4 fusion.44
  351.9 3.4 fusion.43
  355.3 0.3 reduce-scatter.2.cloned.1.call-start
  355.6 82.5 %all-reduce.8.cloned.1.call-done = (f32[1024,448]{0,1:T(8,128)}, f32[1024,448]{0,1:T(8,128)}) async-done(((f32[1024,448]{0,1:T(8,128)}, f32[1024,448]{0,1:T(8,128)}), (f32[1024,448]{0,1:T(8,128)}, f32[1024,448]{0,1:T(8,128)})) %all-reduce.8.cloned.1.call-update) | async-done | bytes 3670032 | tf_op jit(solution)/shard_map/psum | solution.py:150
  438.1 7.7 %fusion.21 = f32[1024,2048]{1,0:T(8,128)} fusion(bf16[448,2048]{1,0:T(8,128)(2,1)S(1)} %copy-done.10, f32[1024,448]{0,1:T(8,128)} %get-tuple-element.231, f32[1024,448]{0,1:T(8,128)} %get-tuple-element.232), kind=kOutput, calls=%fused_computation.41 | convolution fusion | flops 1881800704 | bytes 13893632 | tf_op jit(solution)/shard_map/dot_general | solution.py:153
  445.9 185.7 %reduce-scatter.2.cloned.1.call-done = f32[32,2048]{1,0:T(8,128)} async-done(((f32[1024,2048]{1,0:T(8,128)}), f32[32,2048]{1,0:T(8,128)}) %reduce-scatter.2.cloned.1.call-update) | async-done | bytes 262160 | tf_op jit(solution)/shard_map/reduce_scatter | solution.py:152
  631.5 1.6 add_convert_fusion
  (67 shorter events, 1.1 us)
Async XLA Ops:
  6.5 48.9 %copy-start = (bf16[2,4096,128]{2,1,0:T(8,128)(2,1)S(1)}, bf16[2,4096,128]{2,1,0:T(8,128)(2,1)}, u32[]{:S(2)}) copy-start(bf16[2,4096,128]{2,1,0:T(8,128)(2,1)} %param.24) | copy-start | bytes 6291460
  6.5 150.9 %all-gather.5.cloned.1.call-start = ((), (), s32[]{:S(2)}) async-start(), calls=%async_computation.4 | async-start | bytes 5242880 | tf_op jit(solution)/shard_map/all_gather | solution.py:13
  8.1 16.1 %copy-start.3 = (bf16[256,2048]{1,0:T(8,128)(2,1)S(1)}, bf16[256,2048]{1,0:T(8,128)(2,1)}, u32[]{:S(2)}) copy-start(bf16[256,2048]{1,0:T(8,128)(2,1)} %param.18) | copy-start | bytes 3145732
  8.1 16.1 %copy-start.13 = (f32[2048]{0:T(1024)S(1)}, f32[2048]{0:T(1024)}, u32[]{:S(2)}) copy-start(f32[2048]{0:T(1024)} %param.19) | copy-start | bytes 24580
  19.2 4.9 copy-start.11
  19.2 5.4 copy-start.12
  24.1 28.8 %copy-start.5 = (s32[256]{0:T(256)S(1)}, s32[256]{0:T(256)}, u32[]{:S(2)}) copy-start(s32[256]{0:T(256)} %param.28) | copy-start | bytes 3076
  55.4 14.0 %copy-start.7 = (s32[256]{0:T(256)S(1)}, s32[256]{0:T(256)}, u32[]{:S(2)}) copy-start(s32[256]{0:T(256)} %param.29) | copy-start | bytes 3076
  98.0 178.5 %all-reduce.6.cloned.1.call-start = ((), (), s32[]{:S(2)}) async-start(), calls=%async_computation.2 | async-start | bytes 4194304 | tf_op jit(solution)/shard_map/psum | solution.py:136
  166.8 4.9 copy-start.4
  171.7 266.4 %all-reduce.8.cloned.1.call-start = ((), (), s32[]{:S(2)}) async-start(), calls=%async_computation.5 | async-start | bytes 7340032 | tf_op jit(solution)/shard_map/psum | solution.py:150
  333.8 1.9 copy-start.2
  335.7 9.4 %copy-start.6 = (f32[2048]{0:T(1024)S(1)}, f32[2048]{0:T(1024)}, u32[]{:S(2)}) copy-start(f32[2048]{0:T(1024)} %param.30) | copy-start | bytes 24580
  345.1 3.4 copy-start.8
  348.5 3.4 copy-start.9
  351.9 86.3 %copy-start.10 = (bf16[448,2048]{1,0:T(8,128)(2,1)S(1)}, bf16[448,2048]{1,0:T(8,128)(2,1)}, u32[]{:S(2)}) copy-start(bf16[448,2048]{1,0:T(8,128)(2,1)} %param.33) | copy-start | bytes 5505028
  355.3 276.2 %reduce-scatter.2.cloned.1.call-start = ((), (), s32[]{:S(2)}) async-start(), calls=%async_computation.3 | async-start | bytes 8650752 | tf_op jit(solution)/shard_map/reduce_scatter | solution.py:152
  445.8 187.3 %copy-start.1 = (bf16[2,4096,128]{2,1,0:T(8,128)(2,1)S(1)}, bf16[2,4096,128]{2,1,0:T(8,128)(2,1)}, u32[]{:S(2)}) copy-start(bf16[2,4096,128]{2,1,0:T(8,128)(2,1)} %param.24) | copy-start | bytes 6291460
Sparse Core Ops, SparseCore 0:
  98.1 59.2 all-gather.4
  171.8 104.5 all-reduce.5
  355.4 82.6 all-reduce.7
  446.0 185.5 reduce-scatter.1
